TPU v7x, 32 devices: a whole 2x2x4 slice. The times are simulated.
32 devices in a mesh: dp: 4 (over z), ctx: 8 (over y, x, core).
Axes of the slice: x: 2, y: 2, z: 4, core: 2. Of those that a mesh axis runs over, the one named last changes fastest.
Arguments:
- queries: bfloat16 [4, 1024, 1792], P('dp', 'ctx'), may hold values from -40 to 40
- keys: bfloat16 [4, 1024, 256], P('dp', 'ctx'), may hold values from -8 to 8
- values: bfloat16 [4, 1024, 256], P('dp', 'ctx'), may hold values from -6 to 6
- spikes: int32 [4, 1024, 2], P('dp', 'ctx'), may hold values from 0 to 3
- window_lengths: int32 [2], replicated, may hold values from 128 to 256, as said below
- gain: float32 [1792], replicated, may hold values from 0.1 to 1.9
- cotangent: bfloat16 [4, 1024, 1792], P('dp', 'ctx'), may hold values from -6 to 6
Outputs:
- mixed: bfloat16 [4, 1024, 1792], P('dp', 'ctx')
- d_queries: bfloat16 [4, 1024, 1792], P('dp', 'ctx')
- keys_gradient: bfloat16 [4, 1024, 256], P('dp', 'ctx')
- values_gradient: bfloat16 [4, 1024, 256], P('dp', 'ctx')
- d_gain: float32 [1792], replicated
Inputs may be any that keep to these rules, and one draw needn't show every extreme that they name: `window_lengths`: in every draw one key-value head has a look-back of exactly 256.
All inputs are finite; a program needn't handle non-finite values.
Results may differ from a plain program's by a relative error of at most 0.012.
The roundings to bfloat16 on the way count: a program that leaves them out, or rounds other values in their place, can miss the bound.
Values may be sent and summed in bfloat16 or wider, within the bound.
No kernel may reach another device: no remote copies, remote signals or barrier semaphores. Data moves between devices by JAX's collectives and lax.ppermute only.
A program may use at most 64 MiB of HBM per device.

v0:
```python
import math
import jax
import jax.numpy as jnp
from jax import lax
from jax.sharding import PartitionSpec as P

QUERY_HEADS = 14
KEY_VALUE_HEADS = 2
HEAD_SIZE = 128
WINDOW_REACH = 256
epsilon = 1e-05


def carried_in(part, axis, combine, identity, reverse):
    count = lax.axis_size(axis)
    place = lax.axis_index(axis)
    ahead = count - 1 - place if reverse else place
    gathered = lax.all_gather(part, axis)
    state = jnp.zeros_like(part) + jnp.asarray(identity, part.dtype)

    def one(step, state):
        source = count - 1 - step if reverse else step
        return combine(state, lax.dynamic_index_in_dim(gathered, source, 0, False))

    return lax.fori_loop(0, ahead, one, state)


def shifted(block, axis, distance):
    devices = range(lax.axis_size(axis))
    route = [(i - distance, i) for i in devices if i - distance in devices]
    return lax.ppermute(block, axis, route)


def combine_sum(earlier, later):
    return earlier + later


def per_device(queries, keys, values, spikes, window_lengths, gain, cotangent):
    batch_inputs = queries.shape[0]
    token_rows = queries.shape[1]
    group_size = QUERY_HEADS // KEY_VALUE_HEADS
    reach = (WINDOW_REACH + token_rows - 2) // token_rows
    padding_rows = reach * token_rows
    window_rows = (reach + 1) * token_rows
    scale = HEAD_SIZE ** (-0.5)
    key_value_width = KEY_VALUE_HEADS * HEAD_SIZE
    query_heads = queries.reshape(batch_inputs, token_rows, KEY_VALUE_HEADS, group_size, HEAD_SIZE)
    key_heads = keys.reshape(batch_inputs, token_rows, KEY_VALUE_HEADS, HEAD_SIZE)
    value_heads = values.reshape(batch_inputs, token_rows, KEY_VALUE_HEADS, HEAD_SIZE)
    token_counts = spikes.astype(jnp.float32)[..., None]
    spiked = (value_heads.astype(jnp.float32) * token_counts).astype(jnp.bfloat16)
    local_state = jnp.einsum(
        "nrgd,nrge->ngde", key_heads, spiked, preferred_element_type=jnp.float32
    )
    prior = carried_in(local_state, "ctx", combine_sum, jnp.zeros_like(local_state), False)
    prior_half = prior.astype(jnp.bfloat16)
    earlier = []
    for distance in range(reach, 0, -1):
        earlier.append(shifted((keys, values), "ctx", distance))
    key_window = jnp.concatenate([piece[0] for piece in earlier] + [keys], axis=1).reshape(
        batch_inputs, window_rows, KEY_VALUE_HEADS, HEAD_SIZE
    )
    value_window = jnp.concatenate([piece[1] for piece in earlier] + [values], axis=1).reshape(
        batch_inputs, window_rows, KEY_VALUE_HEADS, HEAD_SIZE
    )
    row_idx = jnp.arange(token_rows)
    causal = (row_idx[:, None] >= row_idx[None, :]).astype(jnp.float32)
    key_idx = jnp.arange(window_rows)
    distance_back = row_idx[:, None] + padding_rows - key_idx[None, :]
    key_pos = lax.axis_index("ctx") * token_rows + key_idx - padding_rows
    visible = (
        (distance_back[None] >= 0)
        & (distance_back[None] < window_lengths[:, None, None])
        & (key_pos >= 0)[None, None, :]
    )
    lin_half = (
        jnp.einsum("nrghd,nsgd->nghrs", query_heads, key_heads, preferred_element_type=jnp.float32)
        * causal
    ).astype(jnp.bfloat16)
    linear = jnp.einsum("nghrs,nsge->nrghe", lin_half, spiked, preferred_element_type=jnp.float32)
    linear = linear + jnp.einsum(
        "nrghd,ngde->nrghe", query_heads, prior_half, preferred_element_type=jnp.float32
    )
    root = jnp.sqrt(jnp.mean(linear * linear, axis=-1, keepdims=True) + epsilon)
    normed = linear / root
    head_gains = gain.reshape(KEY_VALUE_HEADS, group_size, HEAD_SIZE)
    scores = (
        jnp.einsum("nrghd,nmgd->nghrm", query_heads, key_window, preferred_element_type=jnp.float32)
        * scale
    )
    scores = jnp.where(visible[None, :, None], scores, -1e30)
    top = jnp.max(scores, axis=-1, keepdims=True)
    expo = jnp.exp(scores - top)
    probs = expo / jnp.sum(expo, axis=-1, keepdims=True)
    probs_half = probs.astype(jnp.bfloat16)
    window_out = jnp.einsum(
        "nghrm,nmgd->nrghd", probs_half, value_window, preferred_element_type=jnp.float32
    )
    mixed = (
        (head_gains * normed + window_out)
        .astype(jnp.bfloat16)
        .reshape(batch_inputs, token_rows, QUERY_HEADS * HEAD_SIZE)
    )
    head_gradients = cotangent.reshape(
        batch_inputs, token_rows, KEY_VALUE_HEADS, group_size, HEAD_SIZE
    )
    grad_wide = head_gradients.astype(jnp.float32)
    total_tokens = batch_inputs * lax.axis_size("dp") * token_rows * lax.axis_size("ctx")
    gain_local = jnp.sum(grad_wide * normed, axis=(0, 1)).reshape(
        QUERY_HEADS * HEAD_SIZE
    ) / math.sqrt(total_tokens)
    d_gain = lax.psum(gain_local, ("dp", "ctx"))
    scaled = grad_wide * head_gains
    d_linear = (
        (scaled - normed * jnp.mean(scaled * normed, axis=-1, keepdims=True)) / root
    ).astype(jnp.bfloat16)
    suffix_local = jnp.einsum(
        "nrghd,nrghe->ngde", query_heads, d_linear, preferred_element_type=jnp.float32
    )
    later = carried_in(suffix_local, "ctx", combine_sum, jnp.zeros_like(suffix_local), True)
    later_half = later.astype(jnp.bfloat16)
    back_half = (
        jnp.einsum("nrghe,nsge->nghrs", d_linear, spiked, preferred_element_type=jnp.float32)
        * causal
    ).astype(jnp.bfloat16)
    lin_dq = jnp.einsum(
        "nrghe,ngde->nrghd", d_linear, prior_half, preferred_element_type=jnp.float32
    )
    lin_dq = lin_dq + jnp.einsum(
        "nghrs,nsgd->nrghd", back_half, key_heads, preferred_element_type=jnp.float32
    )
    linear_key_gradient = jnp.einsum(
        "nghrs,nrghd->nsgd", back_half, query_heads, preferred_element_type=jnp.float32
    )
    linear_key_gradient = linear_key_gradient + jnp.einsum(
        "nsge,ngde->nsgd", spiked, later_half, preferred_element_type=jnp.float32
    )
    d_spiked = jnp.einsum(
        "nghrs,nrghe->nsge", lin_half, d_linear, preferred_element_type=jnp.float32
    )
    d_spiked = d_spiked + jnp.einsum(
        "nsgd,ngde->nsge", key_heads, later_half, preferred_element_type=jnp.float32
    )
    linear_value_gradient = d_spiked * token_counts
    grad_probs = jnp.einsum(
        "nrghd,nmgd->nghrm", head_gradients, value_window, preferred_element_type=jnp.float32
    )
    delta = jnp.transpose(jnp.sum(grad_wide * window_out, axis=-1), (0, 2, 3, 1))
    grad_scores = (probs * (grad_probs - delta[..., None]) * scale).astype(jnp.bfloat16)
    window_dq = jnp.einsum(
        "nghrm,nmgd->nrghd", grad_scores, key_window, preferred_element_type=jnp.float32
    )
    key_grad_window = jnp.einsum(
        "nghrm,nrghd->nmgd", grad_scores, query_heads, preferred_element_type=jnp.float32
    ).reshape(batch_inputs, window_rows, key_value_width)
    value_grad_window = jnp.einsum(
        "nghrm,nrghd->nmgd", probs_half, head_gradients, preferred_element_type=jnp.float32
    ).reshape(batch_inputs, window_rows, key_value_width)
    received_k = jnp.zeros((batch_inputs, token_rows, key_value_width), jnp.float32)
    received_v = jnp.zeros((batch_inputs, token_rows, key_value_width), jnp.float32)
    for distance in range(1, reach + 1):
        start_row = (reach - distance) * token_rows
        sent_k = key_grad_window[:, start_row : start_row + token_rows]
        sent_v = value_grad_window[:, start_row : start_row + token_rows]
        got_k, got_v = shifted((sent_k, sent_v), "ctx", -distance)
        received_k = received_k + got_k
        received_v = received_v + got_v
    own_k = key_grad_window[:, padding_rows:]
    own_v = value_grad_window[:, padding_rows:]
    d_queries = (
        (lin_dq + window_dq)
        .astype(jnp.bfloat16)
        .reshape(batch_inputs, token_rows, QUERY_HEADS * HEAD_SIZE)
    )
    keys_gradient = (
        linear_key_gradient.reshape(batch_inputs, token_rows, key_value_width) + own_k + received_k
    ).astype(jnp.bfloat16)
    values_gradient = (
        linear_value_gradient.reshape(batch_inputs, token_rows, key_value_width)
        + own_v
        + received_v
    ).astype(jnp.bfloat16)
    return (mixed, d_queries, keys_gradient, values_gradient, d_gain)


def solution(mesh):
    placed = (
        P("dp", "ctx", None),
        P("dp", "ctx", None),
        P("dp", "ctx", None),
        P("dp", "ctx", None),
        P(),
        P(),
        P("dp", "ctx", None),
    )
    return jax.shard_map(
        per_device,
        mesh=mesh,
        in_specs=placed,
        out_specs=(
            P("dp", "ctx", None),
            P("dp", "ctx", None),
            P("dp", "ctx", None),
            P("dp", "ctx", None),
            P(),
        ),
        check_vma=False,
    )
```

profile of v0, /device:TPU:0, one launch (start us, length us, event | category | flops | bytes accessed | tf_op | source)
XLA Modules:
  0.0 137.0 jit_solution(10712127279275393058)
XLA Ops:
  7.2 1.0 copy.113
  8.2 4.8 %collective-permute-start.2 = (bf16[1,128,256]{1,2,0:T(8,128)(2,1)S(1)}, bf16[1,128,256]{1,2,0:T(8,128)(2,1)S(1)}, u32[]{:S(2)}, u32[]{:S(2)}) collective-permute-start(bf16[1,128,256]{1,2,0:T(8,128)(2,1)S(1)} %copy.113), channel_id=1, source_target_pairs={{0,2},{1,3},{2,4},{3,5},{4,6},{5,7},{8,10},{9,11},{10,12},{11,13},... | collective-permute-start | bytes 196616 | tf_op jit(solution)/shard_map/ppermute | solution.py:31
  13.1 1.5 %collective-permute-start.3 = (bf16[1,128,256]{1,2,0:T(8,128)(2,1)S(1)}, bf16[1,128,256]{1,2,0:T(8,128)(2,1)S(1)}, u32[]{:S(2)}, u32[]{:S(2)}) collective-permute-start(bf16[1,128,256]{1,2,0:T(8,128)(2,1)S(1)} %copy.113), channel_id=1, source_target_pairs={{0,1},{1,2},{2,3},{3,4},{4,5},{5,6},{6,7},{8,9},{9,10},{10,11},{11... | collective-permute-start | bytes 196616 | tf_op jit(solution)/shard_map/ppermute | solution.py:31
  14.5 3.9 %collective-permute-start = (bf16[1,128,256]{2,1,0:T(8,128)(2,1)}, bf16[1,128,256]{2,1,0:T(8,128)(2,1)S(1)}, u32[]{:S(2)}, u32[]{:S(2)}) collective-permute-start(bf16[1,128,256]{2,1,0:T(8,128)(2,1)} %param.13), channel_id=1, source_target_pairs={{0,2},{1,3},{2,4},{3,5},{4,6},{5,7},{8,10},{9,11},{10,12},{11,13},... | collective-permute-start | bytes 196616 | tf_op jit(solution)/shard_map/ppermute | solution.py:31
  18.4 3.2 %collective-permute-start.1 = (bf16[1,128,256]{2,1,0:T(8,128)(2,1)}, bf16[1,128,256]{2,1,0:T(8,128)(2,1)S(1)}, u32[]{:S(2)}, u32[]{:S(2)}) collective-permute-start(bf16[1,128,256]{2,1,0:T(8,128)(2,1)} %param.13), channel_id=1, source_target_pairs={{0,1},{1,2},{2,3},{3,4},{4,5},{5,6},{6,7},{8,9},{9,10},{10,11},{11... | collective-permute-start | bytes 196616 | tf_op jit(solution)/shard_map/ppermute | solution.py:31
  21.6 0.9 reshape.302
  22.6 0.9 reshape.284
  23.4 0.7 convert_bitcast_fusion
  24.5 0.8 copy.108
  25.4 1.3 copy.101
  26.9 1.5 %and_and_fusion = pred[2,128,384]{1,2,0:T(8,128)(4,1)} fusion(s32[128,384]{0,1:T(8,128)S(1)} %iota_subtract_fusion, s32[2]{0:T(128)} %param.15, pred[384]{0:T(512)(128)(4,1)S(1)} %add_compare_fusion, pred[128,384]{0,1:T(8,128)(4,1)S(1)} %broadcast_compare_fusion), kind=kLoop, calls=%fused_computation.54 | loop fusion | flops 294912 | bytes 344456 | tf_op jit(solution)/shard_map/and | solution.py:72
  28.3 1.1 fusion.23
  29.5 1.1 copy.119
  30.6 1.0 copy.124
  31.6 0.8 copy.112
  32.5 1.6 %fusion.5 = (f32[2,7,128]{2,1,0:T(8,128)S(1)}, f32[2,384,128,7]{2,1,3,0:T(8,128)S(1)}) fusion(pred[2,128,384]{1,2,0:T(8,128)(4,1)} %and_and_fusion, bf16[384,2,128,1]{0,2,3,1:T(8,128)(2,1)S(1)} %bitcast.263, bf16[128,2,7,128]{0,3,2,1:T(8,128)(2,1)S(1)} %bitcast.255), kind=kOutput, calls=%fused_computation.10 | convolution fusion | flops 178223360 | bytes 3513344 | tf_op jit(solution)/shard_map/nrghd,nmgd->nghrm/dot_general | solution.py:88
  34.7 0.9 fusion.7
  35.6 0.7 fusion.47
  36.4 1.7 %copy.195 = f32[1,128,256]{2,1,0:T(8,128)} copy(f32[1,128,256]{1,2,0:T(8,128)} %get-tuple-element.146) | data formatting | bytes 262144
  38.0 1.3 collective-permute-start.6
  39.3 1.7 %copy.196 = f32[1,128,256]{2,1,0:T(8,128)} copy(f32[1,128,256]{1,2,0:T(8,128)} %get-tuple-element.147) | data formatting | bytes 262144
  41.0 1.3 collective-permute-start.7
  42.3 0.8 copy.194
  43.0 7.1 %all-gather.5.cloned.1.call-done = f32[16,128,128]{2,1,0:T(8,128)} async-done(((f32[2,128,128]{2,1,0:T(8,128)}), f32[16,128,128]{2,1,0:T(8,128)}) %all-gather.5.cloned.1.call-update) | async-done | bytes 1048592 | tf_op jit(solution)/shard_map/all_gather | solution.py:18
  50.5 1.4 %multiply_reduce_fusion.3 = (f32[128,2,7]{0,2,1:T(8,128)S(1)}, f32[1,128,2,7,128]{1,4,3,2,0:T(8,128)S(1)}) fusion(f32[1,128,2,7,128]{1,4,3,2,0:T(8,128)S(1)} %convolution_bitcast_fusion.3, bf16[2,7,128,128]{2,3,1,0:T(8,128)(2,1)} %fusion.23, bf16[128,2,128]{2,0,1:T(8,128)(2,1)} %copy-done.4), kind=kOutput, calls=%fused_computation.48 | convolution fusion | flops 59406592 | bytes 2366464 | tf_op jit(solution)/shard_map/nghrs,nsge->nrghe/dot_general | solution.py:80
  52.0 2.7 %multiply_reduce_fusion = (f32[2,7,128]{2,1,0:T(8,128)}, f32[128,2,7]{0,2,1:T(8,128)S(1)}, f32[128,2,7]{0,2,1:T(8,128)}, bf16[1,128,2,7,128]{1,4,3,2,0:T(8,128)(2,1)}) fusion(f32[1,128,2,7,128]{1,4,3,2,0:T(8,128)S(1)} %bitcast.260, f32[1,128,2,7,128]{1,4,3,2,0:T(8,128)S(1)} %get-tuple-element.152, f32[128,2,7]{0,2,1:T(8,128)S(1)} %add_sqrt_fusion, ...), kind=kOutput, calls=%fused_computation.43 | convolution fusion | flops 182119168 | bytes 5391360 | tf_op jit(solution)/shard_map/nghrm,nmgd->nrghd/dot_general | solution.py:96
  55.3 0.8 copy.130
  56.2 2.9 %fusion.6 = bf16[2,7,128,384]{2,3,1,0:T(8,128)(2,1)S(1)} fusion(bf16[384,2,128,1]{0,2,3,1:T(8,128)(2,1)S(1)} %bitcast.276, bf16[128,2,7,128]{0,3,2,1:T(8,128)(2,1)S(1)} %bitcast.270, f32[2,7,128]{2,1,0:T(8,128)S(1)} %bitcast.277, f32[2,7,128]{2,1,0:T(8,128)S(1)} %copy-done.27, f32[2,7,128]{2,1,0:T(8,128)S(1)} %get-tuple-element.153, ...), kind=kOutput, calls=%fused_computation.11 | convolution fusion | flops 181665792 | bytes 4903936 | tf_op jit(solution)/shard_map/nrghd,nmgd->nghrm/dot_general | solution.py:145
  59.7 0.7 fusion.48
  60.3 1.7 %copy.192 = f32[1,128,256]{2,1,0:T(8,128)} copy(f32[1,128,256]{1,2,0:T(8,128)} %get-tuple-element.149) | data formatting | bytes 262144
  62.0 1.3 collective-permute-start.4
  63.3 0.8 copy.193
  64.0 1.3 collective-permute-start.5
  65.3 0.7 copy.191
  66.9 1.2 fusion.20
  68.1 2.0 %copy.146 = bf16[1,128,1792]{2,1,0:T(8,128)(2,1)} copy(bf16[1,128,1792]{1,2,0:T(8,128)(2,1)} %bitcast.262) | data formatting | bytes 917504
  70.1 2.0 %copy.145 = bf16[1,128,1792]{2,1,0:T(8,128)(2,1)} copy(bf16[1,128,1792]{1,2,0:T(8,128)(2,1)} %bitcast.271) | data formatting | bytes 917504
  72.2 46.7 %psum.7 = f32[1792]{0:T(1024)} all-reduce(f32[1792]{0:T(1024)S(1)} %div.45), channel_id=1, replica_groups=mesh['dp'=4,'ctx'=8] {'dp','ctx'}, use_global_device_ids=true, to_apply=%region_10.11 | all-reduce | flops 1792 | bytes 14336 | tf_op jit(solution)/shard_map/psum | solution.py:112
  119.5 6.8 %while.23 = (s32[]{:T(128)}, f32[1,2,128,128]{3,2,1,0:T(8,128)S(1)}, s32[]{:T(128)}, f32[8,1,2,128,128]{4,3,2,1,0:T(8,128)}, s32[]{:T(128)}, /*index=5*/s32[]{:T(128)}, s32[]{:T(128)}, s32[]{:T(128)}) while((s32[]{:T(128)}, f32[1,2,128,128]{3,2,1,0:T(8,128)S(1)}, s32[]{:T(128)}, f32[8,1,2,128,128]{4,3,2,1,0:T(8,128)}, s32[]{:T(128)}, ...), condition=%wide.region_8.9_spmd, body=%wide.region_7.8_spmd.sunk | while | flops 32774 | bytes 393351 | solution.py:25
  119.5 0.9 bitcast_add_fusion.5
  120.5 0.9 bitcast_add_fusion.5
  121.5 0.9 bitcast_add_fusion.5
  122.4 0.9 bitcast_add_fusion.5
  123.4 0.9 bitcast_add_fusion.5
  124.3 0.9 bitcast_add_fusion.5
  125.3 0.9 bitcast_add_fusion.5
  126.9 1.6 %add_convert_fusion.1 = bf16[1,128,256]{2,1,0:T(8,128)(2,1)} fusion(f32[1,128,256]{2,1,0:T(8,128)} %collective-permute-done.6, f32[1,128,256]{2,1,0:T(8,128)} %collective-permute-done.7, f32[1,128,256]{2,1,0:T(8,128)S(1)} %copy.142, f32[1,128,256]{2,1,0:T(8,128)S(1)} %copy-done.16), kind=kLoop, calls=%fused_computation.60 | loop fusion | flops 131072 | bytes 589824 | tf_op jit(solution)/shard_map/convert_element_type | solution.py:182
  128.6 1.6 %add_convert_fusion.2 = bf16[1,128,256]{2,1,0:T(8,128)(2,1)} fusion(f32[1,128,256]{2,1,0:T(8,128)} %collective-permute-done.4, f32[1,128,256]{2,1,0:T(8,128)} %collective-permute-done.5, f32[1,128,256]{2,1,0:T(8,128)S(1)} %copy.134, f32[1,128,256]{2,1,0:T(8,128)S(1)} %copy-done.17), kind=kLoop, calls=%fused_computation.61 | loop fusion | flops 131072 | bytes 589824 | tf_op jit(solution)/shard_map/convert_element_type | solution.py:177
  (107 shorter events, 5.0 us)
Async XLA Ops:
  7.2 22.3 %copy-start.3 = (bf16[1,128,1792]{2,1,0:T(8,128)(2,1)S(1)}, bf16[1,128,1792]{2,1,0:T(8,128)(2,1)}, u32[]{:S(2)}) copy-start(bf16[1,128,1792]{2,1,0:T(8,128)(2,1)} %param.17) | copy-start | bytes 1376260
  7.2 43.0 %all-gather.5.cloned.1.call-start = ((), (), s32[]{:S(2)}) async-start(), calls=%async_computation | async-start | bytes 1179648 | tf_op jit(solution)/shard_map/all_gather | solution.py:18
  8.2 24.2 %collective-permute-start.2 = (bf16[1,128,256]{1,2,0:T(8,128)(2,1)S(1)}, bf16[1,128,256]{1,2,0:T(8,128)(2,1)S(1)}, u32[]{:S(2)}, u32[]{:S(2)}) collective-permute-start(bf16[1,128,256]{1,2,0:T(8,128)(2,1)S(1)} %copy.113), channel_id=1, source_target_pairs={{0,2},{1,3},{2,4},{3,5},{4,6},{5,7},{8,10},{9,11},{10,12},{11,13},... | collective-permute-start | bytes 196616 | tf_op jit(solution)/shard_map/ppermute | solution.py:31
  13.1 19.4 %collective-permute-start.3 = (bf16[1,128,256]{1,2,0:T(8,128)(2,1)S(1)}, bf16[1,128,256]{1,2,0:T(8,128)(2,1)S(1)}, u32[]{:S(2)}, u32[]{:S(2)}) collective-permute-start(bf16[1,128,256]{1,2,0:T(8,128)(2,1)S(1)} %copy.113), channel_id=1, source_target_pairs={{0,1},{1,2},{2,3},{3,4},{4,5},{5,6},{6,7},{8,9},{9,10},{10,11},{11... | collective-permute-start | bytes 196616 | tf_op jit(solution)/shard_map/ppermute | solution.py:31
  14.5 17.0 %collective-permute-start = (bf16[1,128,256]{2,1,0:T(8,128)(2,1)}, bf16[1,128,256]{2,1,0:T(8,128)(2,1)S(1)}, u32[]{:S(2)}, u32[]{:S(2)}) collective-permute-start(bf16[1,128,256]{2,1,0:T(8,128)(2,1)} %param.13), channel_id=1, source_target_pairs={{0,2},{1,3},{2,4},{3,5},{4,6},{5,7},{8,10},{9,11},{10,12},{11,13},... | collective-permute-start | bytes 196616 | tf_op jit(solution)/shard_map/ppermute | solution.py:31
  18.4 13.2 %collective-permute-start.1 = (bf16[1,128,256]{2,1,0:T(8,128)(2,1)}, bf16[1,128,256]{2,1,0:T(8,128)(2,1)S(1)}, u32[]{:S(2)}, u32[]{:S(2)}) collective-permute-start(bf16[1,128,256]{2,1,0:T(8,128)(2,1)} %param.13), channel_id=1, source_target_pairs={{0,1},{1,2},{2,3},{3,4},{4,5},{5,6},{6,7},{8,9},{9,10},{10,11},{11... | collective-permute-start | bytes 196616 | tf_op jit(solution)/shard_map/ppermute | solution.py:31
  23.4 8.1 %copy-start.7 = (bf16[128,2,128]{2,1,0:T(2,128)(2,1)}, bf16[128,2,128]{2,1,0:T(2,128)(2,1)S(1)}, u32[]{:S(2)}) copy-start(bf16[128,2,128]{2,1,0:T(2,128)(2,1)S(1)} %reshape.284) | copy-start | bytes 196612
  24.1 1.2 copy-start.23
  24.2 1.2 copy-start.4
  24.5 7.1 %copy-start.28 = (f32[1792]{0:T(1024)S(1)}, f32[1792]{0:T(1024)}, u32[]{:S(2)}) copy-start(f32[1792]{0:T(1024)} %param.16) | copy-start | bytes 21508
  24.5 7.1 %copy-start.20 = (bf16[1,128,256]{2,1,0:T(8,128)(2,1)S(1)}, bf16[1,128,256]{2,1,0:T(8,128)(2,1)}, u32[]{:S(2)}) copy-start(bf16[1,128,256]{2,1,0:T(8,128)(2,1)} %param.13) | copy-start | bytes 196612
  25.3 94.2 %all-gather.7.cloned.1.call-start = ((), (), s32[]{:S(2)}) async-start(), calls=%async_computation.1 | async-start | bytes 1179648 | tf_op jit(solution)/shard_map/all_gather | solution.py:18
  26.9 5.6 %copy-start.12 = (bf16[128,2,128,1]{0,2,3,1:T(8,128)(2,1)}, bf16[128,2,128,1]{0,2,3,1:T(8,128)(2,1)S(1)}, u32[]{:S(2)}) copy-start(bf16[128,2,128,1]{0,2,3,1:T(8,128)(2,1)S(1)} %copy.163) | copy-start | bytes 196612
  28.3 4.2 %copy-start.14 = (f32[128,128]{0,1:T(8,128)}, f32[128,128]{0,1:T(8,128)S(1)}, u32[]{:S(2)}) copy-start(f32[128,128]{0,1:T(8,128)S(1)} %fusion.38) | copy-start | bytes 196612
  31.6 2.5 %copy-start.9 = (pred[2,128,384]{1,2,0:T(8,128)(4,1)S(1)}, pred[2,128,384]{1,2,0:T(8,128)(4,1)}, u32[]{:S(2)}) copy-start(pred[2,128,384]{1,2,0:T(8,128)(4,1)} %and_and_fusion) | copy-start | bytes 294916
  32.5 2.2 %copy-start.18 = (bf16[1,128,1792]{1,2,0:T(8,128)(2,1)S(1)}, bf16[1,128,1792]{1,2,0:T(8,128)(2,1)}, u32[]{:S(2)}) copy-start(bf16[1,128,1792]{1,2,0:T(8,128)(2,1)} %copy.124) | copy-start | bytes 1376260
  34.1 17.9 %copy-start = (f32[2,384,128,7]{2,1,3,0:T(8,128)}, f32[2,384,128,7]{2,1,3,0:T(8,128)S(1)}, u32[]{:S(2)}) copy-start(f32[2,384,128,7]{2,1,3,0:T(8,128)S(1)} %get-tuple-element.154) | copy-start | bytes 8257540
  34.7 0.9 copy-start.25
  38.0 88.9 %collective-permute-start.6 = (f32[1,128,256]{2,1,0:T(8,128)}, f32[1,128,256]{2,1,0:T(8,128)}, u32[]{:S(2)}, u32[]{:S(2)}) collective-permute-start(f32[1,128,256]{2,1,0:T(8,128)} %copy.195), channel_id=1, source_target_pairs={{1,0},{2,1},{3,2},{4,3},{5,4},{6,5},{7,6},{9,8},{10,9},{11,10},{12... | collective-permute-start | bytes 393224 | tf_op jit(solution)/shard_map/ppermute | solution.py:31
  41.0 85.9 %collective-permute-start.7 = (f32[1,128,256]{2,1,0:T(8,128)}, f32[1,128,256]{2,1,0:T(8,128)}, u32[]{:S(2)}, u32[]{:S(2)}) collective-permute-start(f32[1,128,256]{2,1,0:T(8,128)} %copy.196), channel_id=1, source_target_pairs={{2,0},{3,1},{4,2},{5,3},{6,4},{7,5},{10,8},{11,9},{12,10},{13,11},... | collective-permute-start | bytes 393224 | tf_op jit(solution)/shard_map/ppermute | solution.py:31
  50.2 1.8 %copy-start.2 = (f32[1,128,1792]{1,2,0:T(8,128)S(1)}, f32[1,128,1792]{1,2,0:T(8,128)}, u32[]{:S(2)}) copy-start(f32[1,128,1792]{1,2,0:T(8,128)} %copy.119) | copy-start | bytes 2752516
  50.2 1.8 %copy-start.10 = (pred[2,128,384]{1,2,0:T(8,128)(4,1)S(1)}, pred[2,128,384]{1,2,0:T(8,128)(4,1)}, u32[]{:S(2)}) copy-start(pred[2,128,384]{1,2,0:T(8,128)(4,1)} %and_and_fusion) | copy-start | bytes 294916
  50.2 1.8 %copy-start.21 = (bf16[1,384,256]{1,2,0:T(8,128)(2,1)S(1)}, bf16[1,384,256]{1,2,0:T(8,128)(2,1)}, u32[]{:S(2)}) copy-start(bf16[1,384,256]{1,2,0:T(8,128)(2,1)} %copy.112) | copy-start | bytes 589828
  50.2 1.8 %copy-start.26 = (f32[2,7,128]{2,1,0:T(8,128)S(1)}, f32[2,7,128]{2,1,0:T(8,128)}, u32[]{:S(2)}) copy-start(f32[2,7,128]{2,1,0:T(8,128)} %copy-done.25) | copy-start | bytes 21508
  54.7 1.4 %copy-start.11 = (pred[2,128,384]{1,2,0:T(8,128)(4,1)S(1)}, pred[2,128,384]{1,2,0:T(8,128)(4,1)}, u32[]{:S(2)}) copy-start(pred[2,128,384]{1,2,0:T(8,128)(4,1)} %and_and_fusion) | copy-start | bytes 294916
  54.7 1.4 %copy-start.19 = (bf16[1,128,1792]{1,2,0:T(8,128)(2,1)S(1)}, bf16[1,128,1792]{1,2,0:T(8,128)(2,1)}, u32[]{:S(2)}) copy-start(bf16[1,128,1792]{1,2,0:T(8,128)(2,1)} %copy.124) | copy-start | bytes 1376260
  54.7 1.4 %copy-start.22 = (bf16[1,384,256]{1,2,0:T(8,128)(2,1)S(1)}, bf16[1,384,256]{1,2,0:T(8,128)(2,1)}, u32[]{:S(2)}) copy-start(bf16[1,384,256]{1,2,0:T(8,128)(2,1)} %copy.112) | copy-start | bytes 589828
  54.7 1.4 %copy-start.27 = (f32[2,7,128]{2,1,0:T(8,128)S(1)}, f32[2,7,128]{2,1,0:T(8,128)}, u32[]{:S(2)}) copy-start(f32[2,7,128]{2,1,0:T(8,128)} %copy-done.25) | copy-start | bytes 21508
  54.7 1.5 %copy-start.30 = (f32[128,2,7]{0,2,1:T(8,128)S(1)}, f32[128,2,7]{0,2,1:T(8,128)}, u32[]{:S(2)}) copy-start(f32[128,2,7]{0,2,1:T(8,128)} %get-tuple-element.127) | copy-start | bytes 21508
  59.1 7.0 %copy-start.5 = (bf16[128,2,128]{2,0,1:T(8,128)(2,1)S(1)}, bf16[128,2,128]{2,0,1:T(8,128)(2,1)}, u32[]{:S(2)}) copy-start(bf16[128,2,128]{2,0,1:T(8,128)(2,1)} %copy-done.4) | copy-start | bytes 196612
  59.1 7.0 %copy-start.15 = (f32[128,128]{0,1:T(8,128)S(1)}, f32[128,128]{0,1:T(8,128)}, u32[]{:S(2)}) copy-start(f32[128,128]{0,1:T(8,128)} %copy-done.14) | copy-start | bytes 196612
  59.1 7.3 %copy-start.13 = (bf16[128,2,128,1]{0,2,3,1:T(8,128)(2,1)S(1)}, bf16[128,2,128,1]{0,2,3,1:T(8,128)(2,1)}, u32[]{:S(2)}) copy-start(bf16[128,2,128,1]{0,2,3,1:T(8,128)(2,1)} %copy-done.12) | copy-start | bytes 196612
  62.0 66.6 %collective-permute-start.4 = (f32[1,128,256]{2,1,0:T(8,128)}, f32[1,128,256]{2,1,0:T(8,128)}, u32[]{:S(2)}, u32[]{:S(2)}) collective-permute-start(f32[1,128,256]{2,1,0:T(8,128)} %copy.192), channel_id=1, source_target_pairs={{1,0},{2,1},{3,2},{4,3},{5,4},{6,5},{7,6},{9,8},{10,9},{11,10},{12... | collective-permute-start | bytes 393224 | tf_op jit(solution)/shard_map/ppermute | solution.py:31
  64.0 64.5 %collective-permute-start.5 = (f32[1,128,256]{2,1,0:T(8,128)}, f32[1,128,256]{2,1,0:T(8,128)}, u32[]{:S(2)}, u32[]{:S(2)}) collective-permute-start(f32[1,128,256]{2,1,0:T(8,128)} %copy.193), channel_id=1, source_target_pairs={{2,0},{3,1},{4,2},{5,3},{6,4},{7,5},{10,8},{11,9},{12,10},{13,11},... | collective-permute-start | bytes 393224 | tf_op jit(solution)/shard_map/ppermute | solution.py:31
  66.9 5.3 %copy-start.29 = (f32[2,7,128]{2,1,0:T(8,128)S(1)}, f32[2,7,128]{2,1,0:T(8,128)}, u32[]{:S(2)}) copy-start(f32[2,7,128]{2,1,0:T(8,128)} %get-tuple-element.125) | copy-start | bytes 21508
  66.9 51.9 %copy-start.1 = (bf16[2,7,128,128]{2,3,1,0:T(8,128)(2,1)S(1)}, bf16[2,7,128,128]{2,3,1,0:T(8,128)(2,1)}, u32[]{:S(2)}) copy-start(bf16[2,7,128,128]{2,3,1,0:T(8,128)(2,1)} %fusion.23) | copy-start | bytes 1376260
  70.1 56.1 %copy-start.8 = (bf16[128,2,128]{2,1,0:T(2,128)(2,1)S(1)}, bf16[128,2,128]{2,1,0:T(2,128)(2,1)}, u32[]{:S(2)}) copy-start(bf16[128,2,128]{2,1,0:T(2,128)(2,1)} %copy-done.7) | copy-start | bytes 196612
  70.1 56.1 %copy-start.24 = (f32[128,2]{0,1:T(2,128)S(1)}, f32[128,2]{0,1:T(2,128)}, u32[]{:S(2)}) copy-start(f32[128,2]{0,1:T(2,128)} %copy-done.23) | copy-start | bytes 3076
  72.2 54.4 %copy-start.6 = (bf16[128,2,128]{2,0,1:T(8,128)(2,1)S(1)}, bf16[128,2,128]{2,0,1:T(8,128)(2,1)}, u32[]{:S(2)}) copy-start(bf16[128,2,128]{2,0,1:T(8,128)(2,1)} %copy-done.4) | copy-start | bytes 196612
  118.8 8.1 %copy-start.16 = (f32[1,128,256]{2,1,0:T(8,128)S(1)}, f32[1,128,256]{2,1,0:T(8,128)}, u32[]{:S(2)}) copy-start(f32[1,128,256]{2,1,0:T(8,128)} %copy.194) | copy-start | bytes 393220
  119.1 9.4 %copy-start.17 = (f32[1,128,256]{2,1,0:T(8,128)S(1)}, f32[1,128,256]{2,1,0:T(8,128)}, u32[]{:S(2)}) copy-start(f32[1,128,256]{2,1,0:T(8,128)} %copy.191) | copy-start | bytes 393220
Sparse Core Ops, SparseCore 0:
  25.4 24.7 all-gather.4
  56.2 32.5 all-gather.6
where the time goes:
time: 138 us; the launch traced here: 137 us
  blocking collectives  46.7 us (34%)
  local copies, waits for them, and re-layouts  21.6 us (16%)
  starting transfers between devices  18.6 us (13%)
  matrix products  14.9 us (11%)
  between operations  14.7 us (11%)
  other arithmetic  13.1 us (9%)
  waiting for transfers between devices  7.19 us (5%)
    psum x1, blocking collectives, per_device(): d_gain = lax.psum(gain_local, ('dp', 'ctx'))  46.7 us
    ppermute x8, starting transfers between devices, shifted(): return lax.ppermute(block, axis, route)  18.5 us
    unnamed x73, local copies, waits for them, and re-layouts  14.6 us
    all_gather x2, waiting for transfers between devices, carried_in(): gathered = lax.all_gather(part, axis)  7.14 us
    add x7, other arithmetic, combine_sum(): return earlier + later  6.56 us
    dot_general x1, matrix products, per_device(): jnp.einsum('nrghd,nmgd->nghrm', head_gradients, value_window, preferred_e...  2.9 us
  transfers between devices with their start and end apart: 10, of which 1 were waited for; matrix products, arithmetic and copies ran while one was open for 34% of the time, Pallas kernels for 0%

commit v1 on v0

--- a/solution.py
+++ b/solution.py
@@ -109,7 +109,7 @@
     gain_local = jnp.sum(grad_wide * normed, axis=(0, 1)).reshape(
         QUERY_HEADS * HEAD_SIZE
     ) / math.sqrt(total_tokens)
-    d_gain = lax.psum(gain_local, ("dp", "ctx"))
+    d_gain = lax.psum(lax.psum(gain_local, "ctx"), "dp")
     scaled = grad_wide * head_gains
     d_linear = (
         (scaled - normed * jnp.mean(scaled * normed, axis=-1, keepdims=True)) / root

time: 138 us -> 126 us (0.913)
  blocking collectives: 46.7 us -> 33.7 us
    psum x1 -> x2, blocking collectives: 46.7 us -> 33.7 us  [per_device(): d_gain = lax.psum(lax.psum(gain_local, 'ctx'), 'dp')]
  transfers between devices with their start and end apart: 10 -> 10, of which waited for: 1 -> 1; matrix products, arithmetic and copies ran while one was open for 34% -> 38% of each run, Pallas kernels for 0% -> 0%
where the time goes in v1:
time: 126 us; the launch traced here: 125 us
  blocking collectives  33.7 us (27%)
  local copies, waits for them, and re-layouts  22.3 us (18%)
  starting transfers between devices  18.6 us (15%)
  matrix products  15 us (12%)
  between operations  14.7 us (12%)
  other arithmetic  13.1 us (10%)
  waiting for transfers between devices  7.17 us (6%)
    psum x2, blocking collectives, per_device(): d_gain = lax.psum(lax.psum(gain_local, 'ctx'), 'dp')  33.7 us
    ppermute x8, starting transfers between devices, shifted(): return lax.ppermute(block, axis, route)  18.5 us
    unnamed x73, local copies, waits for them, and re-layouts  15.3 us
    all_gather x2, waiting for transfers between devices, carried_in(): gathered = lax.all_gather(part, axis)  7.12 us
    add x7, other arithmetic, combine_sum(): return earlier + later  6.56 us
    dot_general x1, matrix products, per_device(): jnp.einsum('nrghd,nmgd->nghrm', head_gradients, value_window, preferred_e...  2.9 us
    dot_general x1, matrix products, per_device(): jnp.einsum('nghrm,nmgd->nrghd', probs_half, value_window, preferred_eleme...  2.67 us
  transfers between devices with their start and end apart: 10, of which 1 were waited for; matrix products, arithmetic and copies ran while one was open for 38% of the time, Pallas kernels for 0%

profile of v1, /device:TPU:0, one launch (start us, length us, event | category | flops | bytes accessed | tf_op | source)
XLA Modules:
  0.0 124.7 jit_solution(10265544468419787564)
XLA Ops:
  7.2 1.0 copy.113
  8.2 4.8 %collective-permute-start.2 = (bf16[1,128,256]{1,2,0:T(8,128)(2,1)S(1)}, bf16[1,128,256]{1,2,0:T(8,128)(2,1)S(1)}, u32[]{:S(2)}, u32[]{:S(2)}) collective-permute-start(bf16[1,128,256]{1,2,0:T(8,128)(2,1)S(1)} %copy.113), channel_id=1, source_target_pairs={{0,2},{1,3},{2,4},{3,5},{4,6},{5,7},{8,10},{9,11},{10,12},{11,13},... | collective-permute-start | bytes 196616 | tf_op jit(solution)/shard_map/ppermute | solution.py:31
  13.1 1.5 %collective-permute-start.3 = (bf16[1,128,256]{1,2,0:T(8,128)(2,1)S(1)}, bf16[1,128,256]{1,2,0:T(8,128)(2,1)S(1)}, u32[]{:S(2)}, u32[]{:S(2)}) collective-permute-start(bf16[1,128,256]{1,2,0:T(8,128)(2,1)S(1)} %copy.113), channel_id=1, source_target_pairs={{0,1},{1,2},{2,3},{3,4},{4,5},{5,6},{6,7},{8,9},{9,10},{10,11},{11... | collective-permute-start | bytes 196616 | tf_op jit(solution)/shard_map/ppermute | solution.py:31
  14.5 3.9 %collective-permute-start = (bf16[1,128,256]{2,1,0:T(8,128)(2,1)}, bf16[1,128,256]{2,1,0:T(8,128)(2,1)S(1)}, u32[]{:S(2)}, u32[]{:S(2)}) collective-permute-start(bf16[1,128,256]{2,1,0:T(8,128)(2,1)} %param.13), channel_id=1, source_target_pairs={{0,2},{1,3},{2,4},{3,5},{4,6},{5,7},{8,10},{9,11},{10,12},{11,13},... | collective-permute-start | bytes 196616 | tf_op jit(solution)/shard_map/ppermute | solution.py:31
  18.4 3.2 %collective-permute-start.1 = (bf16[1,128,256]{2,1,0:T(8,128)(2,1)}, bf16[1,128,256]{2,1,0:T(8,128)(2,1)S(1)}, u32[]{:S(2)}, u32[]{:S(2)}) collective-permute-start(bf16[1,128,256]{2,1,0:T(8,128)(2,1)} %param.13), channel_id=1, source_target_pairs={{0,1},{1,2},{2,3},{3,4},{4,5},{5,6},{6,7},{8,9},{9,10},{10,11},{11... | collective-permute-start | bytes 196616 | tf_op jit(solution)/shard_map/ppermute | solution.py:31
  21.6 0.9 reshape.302
  22.6 0.9 reshape.284
  23.4 0.7 convert_bitcast_fusion
  25.1 0.8 copy.108
  26.0 1.3 %copy.101 = bf16[1,128,1792]{1,2,0:T(8,128)(2,1)S(1)} copy(bf16[1,128,1792]{2,1,0:T(8,128)(2,1)} %param.11) | data formatting | bytes 917504 | tf_op args[0]
  27.5 1.5 %and_and_fusion = pred[2,128,384]{1,2,0:T(8,128)(4,1)} fusion(s32[128,384]{0,1:T(8,128)S(1)} %iota_subtract_fusion, s32[2]{0:T(128)} %param.15, pred[384]{0:T(512)(128)(4,1)S(1)} %add_compare_fusion, pred[128,384]{0,1:T(8,128)(4,1)S(1)} %broadcast_compare_fusion), kind=kLoop, calls=%fused_computation.54 | loop fusion | flops 294912 | bytes 344456 | tf_op jit(solution)/shard_map/and | solution.py:72
  29.0 1.1 fusion.23
  30.1 1.1 copy.119
  31.2 1.0 copy.124
  32.3 0.8 copy.112
  33.2 1.6 %fusion.5 = (f32[2,7,128]{2,1,0:T(8,128)S(1)}, f32[2,384,128,7]{2,1,3,0:T(8,128)S(1)}) fusion(pred[2,128,384]{1,2,0:T(8,128)(4,1)} %and_and_fusion, bf16[384,2,128,1]{0,2,3,1:T(8,128)(2,1)S(1)} %bitcast.263, bf16[128,2,7,128]{0,3,2,1:T(8,128)(2,1)S(1)} %bitcast.255), kind=kOutput, calls=%fused_computation.10 | convolution fusion | flops 178223360 | bytes 3513344 | tf_op jit(solution)/shard_map/nrghd,nmgd->nghrm/dot_general | solution.py:88
  35.3 0.9 fusion.7
  36.3 0.7 fusion.47
  37.0 1.7 %copy.195 = f32[1,128,256]{2,1,0:T(8,128)} copy(f32[1,128,256]{1,2,0:T(8,128)} %get-tuple-element.146) | data formatting | bytes 262144
  38.7 1.3 %collective-permute-start.6 = (f32[1,128,256]{2,1,0:T(8,128)}, f32[1,128,256]{2,1,0:T(8,128)}, u32[]{:S(2)}, u32[]{:S(2)}) collective-permute-start(f32[1,128,256]{2,1,0:T(8,128)} %copy.195), channel_id=1, source_target_pairs={{1,0},{2,1},{3,2},{4,3},{5,4},{6,5},{7,6},{9,8},{10,9},{11,10},{12... | collective-permute-start | bytes 393224 | tf_op jit(solution)/shard_map/ppermute | solution.py:31
  40.0 1.7 %copy.196 = f32[1,128,256]{2,1,0:T(8,128)} copy(f32[1,128,256]{1,2,0:T(8,128)} %get-tuple-element.147) | data formatting | bytes 262144
  41.6 1.3 %collective-permute-start.7 = (f32[1,128,256]{2,1,0:T(8,128)}, f32[1,128,256]{2,1,0:T(8,128)}, u32[]{:S(2)}, u32[]{:S(2)}) collective-permute-start(f32[1,128,256]{2,1,0:T(8,128)} %copy.196), channel_id=1, source_target_pairs={{2,0},{3,1},{4,2},{5,3},{6,4},{7,5},{10,8},{11,9},{12,10},{13,11},... | collective-permute-start | bytes 393224 | tf_op jit(solution)/shard_map/ppermute | solution.py:31
  42.9 0.8 copy.194
  43.6 7.1 %all-gather.5.cloned.1.call-done = f32[16,128,128]{2,1,0:T(8,128)} async-done(((f32[2,128,128]{2,1,0:T(8,128)}), f32[16,128,128]{2,1,0:T(8,128)}) %all-gather.5.cloned.1.call-update) | async-done | bytes 1048592 | tf_op jit(solution)/shard_map/all_gather | solution.py:18
  51.2 1.4 %multiply_reduce_fusion.3 = (f32[128,2,7]{0,2,1:T(8,128)S(1)}, f32[1,128,2,7,128]{1,4,3,2,0:T(8,128)S(1)}) fusion(f32[1,128,2,7,128]{1,4,3,2,0:T(8,128)S(1)} %convolution_bitcast_fusion.3, bf16[2,7,128,128]{2,3,1,0:T(8,128)(2,1)} %fusion.23, bf16[128,2,128]{2,0,1:T(8,128)(2,1)} %copy-done.4), kind=kOutput, calls=%fused_computation.48 | convolution fusion | flops 59406592 | bytes 2366464 | tf_op jit(solution)/shard_map/nghrs,nsge->nrghe/dot_general | solution.py:80
  52.6 2.7 %multiply_reduce_fusion = (f32[2,7,128]{2,1,0:T(8,128)}, f32[128,2,7]{0,2,1:T(8,128)S(1)}, f32[128,2,7]{0,2,1:T(8,128)}, bf16[1,128,2,7,128]{1,4,3,2,0:T(8,128)(2,1)}) fusion(f32[1,128,2,7,128]{1,4,3,2,0:T(8,128)S(1)} %bitcast.260, f32[1,128,2,7,128]{1,4,3,2,0:T(8,128)S(1)} %get-tuple-element.152, f32[128,2,7]{0,2,1:T(8,128)S(1)} %add_sqrt_fusion, ...), kind=kOutput, calls=%fused_computation.43 | convolution fusion | flops 182119168 | bytes 5391360 | tf_op jit(solution)/shard_map/nghrm,nmgd->nrghd/dot_general | solution.py:96
  55.9 0.8 copy.130
  56.8 2.9 %fusion.6 = bf16[2,7,128,384]{2,3,1,0:T(8,128)(2,1)S(1)} fusion(bf16[384,2,128,1]{0,2,3,1:T(8,128)(2,1)S(1)} %bitcast.276, bf16[128,2,7,128]{0,3,2,1:T(8,128)(2,1)S(1)} %bitcast.270, f32[2,7,128]{2,1,0:T(8,128)S(1)} %bitcast.277, f32[2,7,128]{2,1,0:T(8,128)S(1)} %copy-done.27, f32[2,7,128]{2,1,0:T(8,128)S(1)} %get-tuple-element.153, ...), kind=kOutput, calls=%fused_computation.11 | convolution fusion | flops 181665792 | bytes 4903936 | tf_op jit(solution)/shard_map/nrghd,nmgd->nghrm/dot_general | solution.py:145
  60.9 1.7 %copy.192 = f32[1,128,256]{2,1,0:T(8,128)} copy(f32[1,128,256]{1,2,0:T(8,128)} %get-tuple-element.149) | data formatting | bytes 262144
  62.6 1.3 %collective-permute-start.4 = (f32[1,128,256]{2,1,0:T(8,128)}, f32[1,128,256]{2,1,0:T(8,128)}, u32[]{:S(2)}, u32[]{:S(2)}) collective-permute-start(f32[1,128,256]{2,1,0:T(8,128)} %copy.192), channel_id=1, source_target_pairs={{1,0},{2,1},{3,2},{4,3},{5,4},{6,5},{7,6},{9,8},{10,9},{11,10},{12... | collective-permute-start | bytes 393224 | tf_op jit(solution)/shard_map/ppermute | solution.py:31
  63.9 0.8 copy.193
  64.7 1.3 %collective-permute-start.5 = (f32[1,128,256]{2,1,0:T(8,128)}, f32[1,128,256]{2,1,0:T(8,128)}, u32[]{:S(2)}, u32[]{:S(2)}) collective-permute-start(f32[1,128,256]{2,1,0:T(8,128)} %copy.193), channel_id=1, source_target_pairs={{2,0},{3,1},{4,2},{5,3},{6,4},{7,5},{10,8},{11,9},{12,10},{13,11},... | collective-permute-start | bytes 393224 | tf_op jit(solution)/shard_map/ppermute | solution.py:31
  65.9 0.8 copy.191
  67.6 1.2 fusion.20
  68.8 2.0 %copy.146 = bf16[1,128,1792]{2,1,0:T(8,128)(2,1)} copy(bf16[1,128,1792]{1,2,0:T(8,128)(2,1)} %bitcast.262) | data formatting | bytes 917504
  70.8 2.0 %copy.145 = bf16[1,128,1792]{2,1,0:T(8,128)(2,1)} copy(bf16[1,128,1792]{1,2,0:T(8,128)(2,1)} %bitcast.271) | data formatting | bytes 917504
  72.8 21.2 %psum.14 = f32[1792]{0:T(1024)S(1)} all-reduce(f32[1792]{0:T(1024)S(1)} %div.45), channel_id=1, replica_groups=mesh['dp'=4,'ctx'=8] {'ctx'}, use_global_device_ids=true, to_apply=%region_10.11 | all-reduce | flops 1792 | bytes 14336 | tf_op jit(solution)/shard_map/psum | solution.py:112
  94.1 12.4 %psum.15 = f32[1792]{0:T(1024)} all-reduce(f32[1792]{0:T(1024)S(1)} %psum.14), channel_id=1, replica_groups=mesh['dp'=4,'ctx'=8] {'dp'}, use_global_device_ids=true, to_apply=%region_11.12 | all-reduce | flops 1792 | bytes 14336 | tf_op jit(solution)/shard_map/psum | solution.py:112
  107.2 6.8 %while.23 = (s32[]{:T(128)}, f32[1,2,128,128]{3,2,1,0:T(8,128)S(1)}, s32[]{:T(128)}, f32[8,1,2,128,128]{4,3,2,1,0:T(8,128)}, s32[]{:T(128)}, /*index=5*/s32[]{:T(128)}, s32[]{:T(128)}, s32[]{:T(128)}) while((s32[]{:T(128)}, f32[1,2,128,128]{3,2,1,0:T(8,128)S(1)}, s32[]{:T(128)}, f32[8,1,2,128,128]{4,3,2,1,0:T(8,128)}, s32[]{:T(128)}, ...), condition=%wide.region_8.9_spmd, body=%wide.region_7.8_spmd.sunk | while | flops 32774 | bytes 393351 | solution.py:25
  107.2 0.9 bitcast_add_fusion.5
  108.1 0.9 bitcast_add_fusion.5
  109.1 0.9 bitcast_add_fusion.5
  110.1 0.9 bitcast_add_fusion.5
  111.0 0.9 bitcast_add_fusion.5
  112.0 0.9 bitcast_add_fusion.5
  113.0 0.9 bitcast_add_fusion.5
  114.6 1.6 %add_convert_fusion.1 = bf16[1,128,256]{2,1,0:T(8,128)(2,1)} fusion(f32[1,128,256]{2,1,0:T(8,128)} %collective-permute-done.6, f32[1,128,256]{2,1,0:T(8,128)} %collective-permute-done.7, f32[1,128,256]{2,1,0:T(8,128)S(1)} %copy.142, f32[1,128,256]{2,1,0:T(8,128)S(1)} %copy-done.16), kind=kLoop, calls=%fused_computation.60 | loop fusion | flops 131072 | bytes 589824 | tf_op jit(solution)/shard_map/convert_element_type | solution.py:182
  116.2 1.6 %add_convert_fusion.2 = bf16[1,128,256]{2,1,0:T(8,128)(2,1)} fusion(f32[1,128,256]{2,1,0:T(8,128)} %collective-permute-done.4, f32[1,128,256]{2,1,0:T(8,128)} %collective-permute-done.5, f32[1,128,256]{2,1,0:T(8,128)S(1)} %copy.134, f32[1,128,256]{2,1,0:T(8,128)S(1)} %copy-done.17), kind=kLoop, calls=%fused_computation.61 | loop fusion | flops 131072 | bytes 589824 | tf_op jit(solution)/shard_map/convert_element_type | solution.py:177
  (108 shorter events, 6.3 us)
Async XLA Ops:
  7.2 22.9 %copy-start.3 = (bf16[1,128,1792]{2,1,0:T(8,128)(2,1)S(1)}, bf16[1,128,1792]{2,1,0:T(8,128)(2,1)}, u32[]{:S(2)}) copy-start(bf16[1,128,1792]{2,1,0:T(8,128)(2,1)} %param.17) | copy-start | bytes 1376260
  7.2 43.6 %all-gather.5.cloned.1.call-start = ((), (), s32[]{:S(2)}) async-start(), calls=%async_computation | async-start | bytes 1179648 | tf_op jit(solution)/shard_map/all_gather | solution.py:18
  8.2 24.9 %collective-permute-start.2 = (bf16[1,128,256]{1,2,0:T(8,128)(2,1)S(1)}, bf16[1,128,256]{1,2,0:T(8,128)(2,1)S(1)}, u32[]{:S(2)}, u32[]{:S(2)}) collective-permute-start(bf16[1,128,256]{1,2,0:T(8,128)(2,1)S(1)} %copy.113), channel_id=1, source_target_pairs={{0,2},{1,3},{2,4},{3,5},{4,6},{5,7},{8,10},{9,11},{10,12},{11,13},... | collective-permute-start | bytes 196616 | tf_op jit(solution)/shard_map/ppermute | solution.py:31
  13.1 20.0 %collective-permute-start.3 = (bf16[1,128,256]{1,2,0:T(8,128)(2,1)S(1)}, bf16[1,128,256]{1,2,0:T(8,128)(2,1)S(1)}, u32[]{:S(2)}, u32[]{:S(2)}) collective-permute-start(bf16[1,128,256]{1,2,0:T(8,128)(2,1)S(1)} %copy.113), channel_id=1, source_target_pairs={{0,1},{1,2},{2,3},{3,4},{4,5},{5,6},{6,7},{8,9},{9,10},{10,11},{11... | collective-permute-start | bytes 196616 | tf_op jit(solution)/shard_map/ppermute | solution.py:31
  14.5 17.7 %collective-permute-start = (bf16[1,128,256]{2,1,0:T(8,128)(2,1)}, bf16[1,128,256]{2,1,0:T(8,128)(2,1)S(1)}, u32[]{:S(2)}, u32[]{:S(2)}) collective-permute-start(bf16[1,128,256]{2,1,0:T(8,128)(2,1)} %param.13), channel_id=1, source_target_pairs={{0,2},{1,3},{2,4},{3,5},{4,6},{5,7},{8,10},{9,11},{10,12},{11,13},... | collective-permute-start | bytes 196616 | tf_op jit(solution)/shard_map/ppermute | solution.py:31
  18.4 13.8 %collective-permute-start.1 = (bf16[1,128,256]{2,1,0:T(8,128)(2,1)}, bf16[1,128,256]{2,1,0:T(8,128)(2,1)S(1)}, u32[]{:S(2)}, u32[]{:S(2)}) collective-permute-start(bf16[1,128,256]{2,1,0:T(8,128)(2,1)} %param.13), channel_id=1, source_target_pairs={{0,1},{1,2},{2,3},{3,4},{4,5},{5,6},{6,7},{8,9},{9,10},{10,11},{11... | collective-permute-start | bytes 196616 | tf_op jit(solution)/shard_map/ppermute | solution.py:31
  23.4 8.8 %copy-start.7 = (bf16[128,2,128]{2,1,0:T(2,128)(2,1)}, bf16[128,2,128]{2,1,0:T(2,128)(2,1)S(1)}, u32[]{:S(2)}) copy-start(bf16[128,2,128]{2,1,0:T(2,128)(2,1)S(1)} %reshape.284) | copy-start | bytes 196612
  24.1 1.8 %copy-start.23 = (f32[128,2]{0,1:T(2,128)}, f32[128,2]{0,1:T(2,128)S(1)}, u32[]{:S(2)}) copy-start(f32[128,2]{0,1:T(2,128)S(1)} %convert_bitcast_fusion) | copy-start | bytes 3076
  24.2 0.6 copy-start.4
  25.1 7.1 %copy-start.28 = (f32[1792]{0:T(1024)S(1)}, f32[1792]{0:T(1024)}, u32[]{:S(2)}) copy-start(f32[1792]{0:T(1024)} %param.16) | copy-start | bytes 21508
  25.1 7.1 %copy-start.20 = (bf16[1,128,256]{2,1,0:T(8,128)(2,1)S(1)}, bf16[1,128,256]{2,1,0:T(8,128)(2,1)}, u32[]{:S(2)}) copy-start(bf16[1,128,256]{2,1,0:T(8,128)(2,1)} %param.13) | copy-start | bytes 196612
  25.9 81.2 %all-gather.7.cloned.1.call-start = ((), (), s32[]{:S(2)}) async-start(), calls=%async_computation.1 | async-start | bytes 1179648 | tf_op jit(solution)/shard_map/all_gather | solution.py:18
  27.5 5.7 %copy-start.12 = (bf16[128,2,128,1]{0,2,3,1:T(8,128)(2,1)}, bf16[128,2,128,1]{0,2,3,1:T(8,128)(2,1)S(1)}, u32[]{:S(2)}) copy-start(bf16[128,2,128,1]{0,2,3,1:T(8,128)(2,1)S(1)} %copy.163) | copy-start | bytes 196612
  29.0 4.2 %copy-start.14 = (f32[128,128]{0,1:T(8,128)}, f32[128,128]{0,1:T(8,128)S(1)}, u32[]{:S(2)}) copy-start(f32[128,128]{0,1:T(8,128)S(1)} %fusion.38) | copy-start | bytes 196612
  32.2 2.5 %copy-start.9 = (pred[2,128,384]{1,2,0:T(8,128)(4,1)S(1)}, pred[2,128,384]{1,2,0:T(8,128)(4,1)}, u32[]{:S(2)}) copy-start(pred[2,128,384]{1,2,0:T(8,128)(4,1)} %and_and_fusion) | copy-start | bytes 294916
  33.1 2.2 %copy-start.18 = (bf16[1,128,1792]{1,2,0:T(8,128)(2,1)S(1)}, bf16[1,128,1792]{1,2,0:T(8,128)(2,1)}, u32[]{:S(2)}) copy-start(bf16[1,128,1792]{1,2,0:T(8,128)(2,1)} %copy.124) | copy-start | bytes 1376260
  34.7 17.9 %copy-start = (f32[2,384,128,7]{2,1,3,0:T(8,128)}, f32[2,384,128,7]{2,1,3,0:T(8,128)S(1)}, u32[]{:S(2)}) copy-start(f32[2,384,128,7]{2,1,3,0:T(8,128)S(1)} %get-tuple-element.154) | copy-start | bytes 8257540
  35.3 0.9 copy-start.25
  38.7 75.9 %collective-permute-start.6 = (f32[1,128,256]{2,1,0:T(8,128)}, f32[1,128,256]{2,1,0:T(8,128)}, u32[]{:S(2)}, u32[]{:S(2)}) collective-permute-start(f32[1,128,256]{2,1,0:T(8,128)} %copy.195), channel_id=1, source_target_pairs={{1,0},{2,1},{3,2},{4,3},{5,4},{6,5},{7,6},{9,8},{10,9},{11,10},{12... | collective-permute-start | bytes 393224 | tf_op jit(solution)/shard_map/ppermute | solution.py:31
  41.6 73.0 %collective-permute-start.7 = (f32[1,128,256]{2,1,0:T(8,128)}, f32[1,128,256]{2,1,0:T(8,128)}, u32[]{:S(2)}, u32[]{:S(2)}) collective-permute-start(f32[1,128,256]{2,1,0:T(8,128)} %copy.196), channel_id=1, source_target_pairs={{2,0},{3,1},{4,2},{5,3},{6,4},{7,5},{10,8},{11,9},{12,10},{13,11},... | collective-permute-start | bytes 393224 | tf_op jit(solution)/shard_map/ppermute | solution.py:31
  50.8 1.8 %copy-start.2 = (f32[1,128,1792]{1,2,0:T(8,128)S(1)}, f32[1,128,1792]{1,2,0:T(8,128)}, u32[]{:S(2)}) copy-start(f32[1,128,1792]{1,2,0:T(8,128)} %copy.119) | copy-start | bytes 2752516
  50.8 1.8 %copy-start.10 = (pred[2,128,384]{1,2,0:T(8,128)(4,1)S(1)}, pred[2,128,384]{1,2,0:T(8,128)(4,1)}, u32[]{:S(2)}) copy-start(pred[2,128,384]{1,2,0:T(8,128)(4,1)} %and_and_fusion) | copy-start | bytes 294916
  50.8 1.8 %copy-start.21 = (bf16[1,384,256]{1,2,0:T(8,128)(2,1)S(1)}, bf16[1,384,256]{1,2,0:T(8,128)(2,1)}, u32[]{:S(2)}) copy-start(bf16[1,384,256]{1,2,0:T(8,128)(2,1)} %copy.112) | copy-start | bytes 589828
  50.8 1.8 %copy-start.26 = (f32[2,7,128]{2,1,0:T(8,128)S(1)}, f32[2,7,128]{2,1,0:T(8,128)}, u32[]{:S(2)}) copy-start(f32[2,7,128]{2,1,0:T(8,128)} %copy-done.25) | copy-start | bytes 21508
  55.3 1.4 %copy-start.11 = (pred[2,128,384]{1,2,0:T(8,128)(4,1)S(1)}, pred[2,128,384]{1,2,0:T(8,128)(4,1)}, u32[]{:S(2)}) copy-start(pred[2,128,384]{1,2,0:T(8,128)(4,1)} %and_and_fusion) | copy-start | bytes 294916
  55.3 1.4 %copy-start.19 = (bf16[1,128,1792]{1,2,0:T(8,128)(2,1)S(1)}, bf16[1,128,1792]{1,2,0:T(8,128)(2,1)}, u32[]{:S(2)}) copy-start(bf16[1,128,1792]{1,2,0:T(8,128)(2,1)} %copy.124) | copy-start | bytes 1376260
  55.3 1.4 %copy-start.22 = (bf16[1,384,256]{1,2,0:T(8,128)(2,1)S(1)}, bf16[1,384,256]{1,2,0:T(8,128)(2,1)}, u32[]{:S(2)}) copy-start(bf16[1,384,256]{1,2,0:T(8,128)(2,1)} %copy.112) | copy-start | bytes 589828
  55.3 1.5 %copy-start.27 = (f32[2,7,128]{2,1,0:T(8,128)S(1)}, f32[2,7,128]{2,1,0:T(8,128)}, u32[]{:S(2)}) copy-start(f32[2,7,128]{2,1,0:T(8,128)} %copy-done.25) | copy-start | bytes 21508
  55.3 1.5 %copy-start.30 = (f32[128,2,7]{0,2,1:T(8,128)S(1)}, f32[128,2,7]{0,2,1:T(8,128)}, u32[]{:S(2)}) copy-start(f32[128,2,7]{0,2,1:T(8,128)} %get-tuple-element.127) | copy-start | bytes 21508
  59.7 7.0 %copy-start.5 = (bf16[128,2,128]{2,0,1:T(8,128)(2,1)S(1)}, bf16[128,2,128]{2,0,1:T(8,128)(2,1)}, u32[]{:S(2)}) copy-start(bf16[128,2,128]{2,0,1:T(8,128)(2,1)} %copy-done.4) | copy-start | bytes 196612
  59.7 7.0 %copy-start.15 = (f32[128,128]{0,1:T(8,128)S(1)}, f32[128,128]{0,1:T(8,128)}, u32[]{:S(2)}) copy-start(f32[128,128]{0,1:T(8,128)} %copy-done.14) | copy-start | bytes 196612
  59.7 7.3 %copy-start.13 = (bf16[128,2,128,1]{0,2,3,1:T(8,128)(2,1)S(1)}, bf16[128,2,128,1]{0,2,3,1:T(8,128)(2,1)}, u32[]{:S(2)}) copy-start(bf16[128,2,128,1]{0,2,3,1:T(8,128)(2,1)} %copy-done.12) | copy-start | bytes 196612
  62.6 53.6 %collective-permute-start.4 = (f32[1,128,256]{2,1,0:T(8,128)}, f32[1,128,256]{2,1,0:T(8,128)}, u32[]{:S(2)}, u32[]{:S(2)}) collective-permute-start(f32[1,128,256]{2,1,0:T(8,128)} %copy.192), channel_id=1, source_target_pairs={{1,0},{2,1},{3,2},{4,3},{5,4},{6,5},{7,6},{9,8},{10,9},{11,10},{12... | collective-permute-start | bytes 393224 | tf_op jit(solution)/shard_map/ppermute | solution.py:31
  64.7 51.6 %collective-permute-start.5 = (f32[1,128,256]{2,1,0:T(8,128)}, f32[1,128,256]{2,1,0:T(8,128)}, u32[]{:S(2)}, u32[]{:S(2)}) collective-permute-start(f32[1,128,256]{2,1,0:T(8,128)} %copy.193), channel_id=1, source_target_pairs={{2,0},{3,1},{4,2},{5,3},{6,4},{7,5},{10,8},{11,9},{12,10},{13,11},... | collective-permute-start | bytes 393224 | tf_op jit(solution)/shard_map/ppermute | solution.py:31
  67.5 5.3 %copy-start.29 = (f32[2,7,128]{2,1,0:T(8,128)S(1)}, f32[2,7,128]{2,1,0:T(8,128)}, u32[]{:S(2)}) copy-start(f32[2,7,128]{2,1,0:T(8,128)} %get-tuple-element.125) | copy-start | bytes 21508
  67.5 38.9 %copy-start.1 = (bf16[2,7,128,128]{2,3,1,0:T(8,128)(2,1)S(1)}, bf16[2,7,128,128]{2,3,1,0:T(8,128)(2,1)}, u32[]{:S(2)}) copy-start(bf16[2,7,128,128]{2,3,1,0:T(8,128)(2,1)} %fusion.23) | copy-start | bytes 1376260
  70.8 43.1 %copy-start.8 = (bf16[128,2,128]{2,1,0:T(2,128)(2,1)S(1)}, bf16[128,2,128]{2,1,0:T(2,128)(2,1)}, u32[]{:S(2)}) copy-start(bf16[128,2,128]{2,1,0:T(2,128)(2,1)} %copy-done.7) | copy-start | bytes 196612
  70.8 43.2 %copy-start.24 = (f32[128,2]{0,1:T(2,128)S(1)}, f32[128,2]{0,1:T(2,128)}, u32[]{:S(2)}) copy-start(f32[128,2]{0,1:T(2,128)} %copy-done.23) | copy-start | bytes 3076
  72.8 41.5 %copy-start.6 = (bf16[128,2,128]{2,0,1:T(8,128)(2,1)S(1)}, bf16[128,2,128]{2,0,1:T(8,128)(2,1)}, u32[]{:S(2)}) copy-start(bf16[128,2,128]{2,0,1:T(8,128)(2,1)} %copy-done.4) | copy-start | bytes 196612
  106.5 8.1 %copy-start.16 = (f32[1,128,256]{2,1,0:T(8,128)S(1)}, f32[1,128,256]{2,1,0:T(8,128)}, u32[]{:S(2)}) copy-start(f32[1,128,256]{2,1,0:T(8,128)} %copy.194) | copy-start | bytes 393220
  106.8 9.4 %copy-start.17 = (f32[1,128,256]{2,1,0:T(8,128)S(1)}, f32[1,128,256]{2,1,0:T(8,128)}, u32[]{:S(2)}) copy-start(f32[1,128,256]{2,1,0:T(8,128)} %copy.191) | copy-start | bytes 393220
Sparse Core Ops, SparseCore 0:
  26.0 24.7 all-gather.4
  56.8 32.2 all-gather.6
